TPU v7x, 32 devices: a whole 2x2x4 slice. The times are simulated.
32 devices in a mesh: box: 8 (over z, y), dir: 4 (over x, core).
Axes of the slice: x: 2, y: 2, z: 4, core: 2. Of those that a mesh axis runs over, the one named last changes fastest.
Arguments:
- child_pattern: float32 [1024, 4, 128, 128], P('box', None, 'dir'), may hold values from -5 to 5
- octant: int32 [1024], P('box'), may hold values from 0 to 7, as said below
- shift_angle: float32 [8, 256, 256], replicated, may hold values from -3.140625 to 3.140625
- trans_table: bfloat16 [316, 2, 256, 256], P(None, None, 'dir'), may hold values from -2 to 2
- pair_near: int32 [1536], P('box'), may hold values from 0 to 15, as said below
- pair_far: int32 [1536], P('box'), may hold values from 0 to 47, as said below
- pair_class: int32 [1536], P('box'), may hold values from 0 to 315
- pair_live: int32 [1536], P('box'), may hold values from 0 to 1, as said below
Outputs:
- aggregated: float32 [128, 4, 256, 256], P('box', None, 'dir')
- incoming: float32 [128, 4, 256, 256], P('box', None, 'dir')
Inputs may be any that keep to these rules, and one draw needn't show every extreme that they name: `octant`: within each parent's eight consecutive children, a permutation of 0 to 7. `pair_near`: index of the pair's first box among the 16 boxes of the device that holds the slot. `pair_far`: index into the boxes of the slot's own device followed by those of the next 2 devices along box; never the pair's first box, never past the last box. `pair_live`: each device's live slots come first; some device has all 192 slots live.
All inputs are finite; a program needn't handle non-finite values.
Results may differ from a plain program's by a relative error of at most 0.0003.
Values sent between devices are 32-bit elements; how exact they have to be, the bound alone decides.
No kernel may reach another device: no remote copies, remote signals or barrier semaphores. Data moves between devices by JAX's collectives and lax.ppermute only.
A program may use at most 384 MiB of HBM per device.

v0:
```python
import math

import jax
import jax.numpy as jnp
from jax import lax
from jax.sharding import PartitionSpec as P

BOX_DEV = 16
REACH = 2
CLASSES = 316
THETA1 = 128
PHI1 = 128
THETA2 = 256
PHI2 = 256


HIGHEST = lax.Precision.HIGHEST


def passed_along(value, axis, steps):
    count = lax.axis_size(axis)
    first, last = (max(0, -steps), min(count, count - steps))
    return lax.ppermute(value, axis, [(source, source + steps) for source in range(first, last)])


def interp_rows(size_in, size_out, count):
    target_pos = jnp.arange(count, dtype=jnp.int32)
    source_pos = jnp.arange(size_in, dtype=jnp.int32)
    offset = target_pos[:, None] - 2 * source_pos[None, :]
    is_odd = offset % 2 == 1
    safe_off = jnp.where(is_odd, offset, 1).astype(jnp.float32)
    kernel = jnp.sin(math.pi * safe_off / 2.0) / (size_in * jnp.tan(math.pi * safe_off / size_out))
    inner = jnp.where(is_odd, kernel, jnp.zeros_like(kernel))
    return jnp.where(offset == 0, jnp.ones_like(kernel), inner)


def interpolate(fields, theta_map, phi_map):
    widened = jnp.einsum("...t,ut->...u", fields, theta_map, precision=HIGHEST)
    return jnp.einsum("qp,...pu->...qu", phi_map, widened, precision=HIGHEST)


def select_rows(indices, table):
    count = table.shape[0]
    flat_ids = indices.reshape(-1)
    row_ids = jnp.arange(count, dtype=jnp.int32)
    onehot = (flat_ids[:, None] == row_ids[None, :]).astype(table.dtype)
    flat_table = table.reshape(count, -1)
    if table.dtype == jnp.float32:
        picked = jnp.dot(onehot, flat_table, precision=HIGHEST, preferred_element_type=jnp.float32)
    else:
        picked = jnp.dot(onehot, flat_table, preferred_element_type=jnp.float32)
    return picked.reshape(indices.shape + table.shape[1:])


def shift_sum(fields, octant_rows, cos_table, sin_table):
    groups = fields.shape[0]
    cosine = select_rows(octant_rows, cos_table)[:, :, None]
    sine = select_rows(octant_rows, sin_table)[:, :, None]
    shaped = fields.reshape(groups, 8, 2, 2, fields.shape[3], fields.shape[4])
    real_part = shaped[:, :, :, 0]
    imag_part = shaped[:, :, :, 1]
    new_real = jnp.sum(cosine * real_part - sine * imag_part, axis=1)
    new_imag = jnp.sum(sine * real_part + cosine * imag_part, axis=1)
    return jnp.stack([new_real, new_imag], axis=2).reshape(
        groups, 4, fields.shape[3], fields.shape[4]
    )


def translate(table_rows, patterns):
    shaped = patterns.reshape(patterns.shape[:-3] + (2, 2) + patterns.shape[-2:])
    t_real = table_rows[..., 0:1, :, :]
    t_imag = table_rows[..., 1:2, :, :]
    p_real = shaped[..., :, 0, :, :]
    p_imag = shaped[..., :, 1, :, :]
    new_real = t_real * p_real - t_imag * p_imag
    new_imag = t_imag * p_real + t_real * p_imag
    return jnp.stack([new_real, new_imag], axis=-3).reshape(patterns.shape)


def collect(targets, weights, terms, count):
    target_ids = jnp.arange(count, dtype=jnp.int32)
    onehot = jnp.where(targets[None, :] == target_ids[:, None], weights[None, :], 0.0)
    return jnp.dot(onehot, terms.reshape(terms.shape[0], -1), precision=HIGHEST)


def body(
    child_pattern, octant, shift_angle, trans_table, pair_near, pair_far, pair_class, pair_live
):
    dir_count = lax.axis_size("dir")
    dir_index = lax.axis_index("dir")
    theta_map = interp_rows(THETA1, THETA2, THETA2)
    cos_table = jnp.cos(shift_angle)
    sin_table = jnp.sin(shift_angle)
    grouped = child_pattern.reshape(BOX_DEV, 8, 4, PHI1 // dir_count, THETA1)
    gathered = lax.all_to_all(grouped, "dir", split_axis=0, concat_axis=3, tiled=True)
    per_dev = BOX_DEV // dir_count
    octant_rows = lax.dynamic_slice_in_dim(octant, dir_index * (per_dev * 8), per_dev * 8).reshape(
        per_dev, 8
    )
    phi_map = interp_rows(PHI1, PHI2, PHI2)
    full_dirs = interpolate(gathered, theta_map, phi_map)
    summed = shift_sum(full_dirs, octant_rows, cos_table, sin_table)
    aggregated = lax.all_to_all(summed, "dir", split_axis=2, concat_axis=0, tiled=True)
    table_near = select_rows(pair_class, trans_table)
    mirror = (pair_class + CLASSES // 2) % CLASSES
    table_far = select_rows(mirror, trans_table)
    alive = pair_live.astype(jnp.float32)
    to_far = translate(table_far, select_rows(pair_near, aggregated))
    blocks = [aggregated]
    for offset in range(1, REACH + 1):
        blocks.append(passed_along(aggregated, "box", -offset))
    window = jnp.concatenate(blocks, axis=0)
    to_near = translate(table_near, select_rows(pair_far, window))
    incoming = collect(pair_near, alive, to_near, BOX_DEV).reshape(aggregated.shape)
    spread = collect(pair_far, alive, to_far, (REACH + 1) * BOX_DEV).reshape(
        (REACH + 1) * BOX_DEV, *aggregated.shape[1:]
    )
    incoming = incoming + spread[:BOX_DEV]
    for offset in range(1, REACH + 1):
        incoming = incoming + passed_along(
            spread[offset * BOX_DEV : (offset + 1) * BOX_DEV], "box", offset
        )
    return (aggregated, incoming)


def solution(mesh):
    placed = (
        P("box", None, "dir", None),
        P("box"),
        P(),
        P(None, None, "dir", None),
        P("box"),
        P("box"),
        P("box"),
        P("box"),
    )
    return jax.shard_map(
        body,
        mesh=mesh,
        in_specs=placed,
        out_specs=(P("box", None, "dir", None), P("box", None, "dir", None)),
        check_vma=False,
    )
```

profile of v0, /device:TPU:22, one launch (start us, length us, event | category | flops | bytes accessed | tf_op | source)
XLA Modules:
  0.0 716.8 jit_solution(3732084748117311785)
XLA Ops:
  0.6 6.2 all-to-all-start
  7.0 8.4 %cosine_bitcast_fusion = (f32[1,8,256,256]{3,2,1,0:T(8,128)S(1)}, f32[1,8,256,256]{3,2,1,0:T(8,128)S(1)}) fusion(f32[8,256,256]{2,1,0:T(8,128)} %param.10), kind=kLoop, calls=%fused_computation.32 | loop fusion | bytes 6291456
  15.4 5.9 fusion.42
  21.2 9.9 %copy.48 = f32[4,8,256,256]{2,3,1,0:T(8,128)} copy(f32[4,8,256,256]{3,1,2,0:T(8,128)} %fusion.42) | data formatting | bytes 16777216 | tf_op jit(solution)/shard_map/dot_general | solution.py:49
  31.2 5.8 fusion.44
  37.0 9.9 %copy.45 = f32[4,8,256,256]{2,3,1,0:T(8,128)} copy(f32[4,8,256,256]{3,1,2,0:T(8,128)} %fusion.44) | data formatting | bytes 16777216 | tf_op jit(solution)/shard_map/dot_general | solution.py:49
  48.2 26.7 %fusion.2 = f32[192,2,64,256]{3,0,2,1:T(8,128)} fusion(bf16[2,64,256,316]{2,1,0,3:T(8,128)(2,1)} %bitcast.171, s32[192]{0:T(256)S(1)} %and_select_fusion), kind=kOutput, calls=%fused_computation.8 | convolution fusion | flops 3976260864 | bytes 45875968 | tf_op jit(solution)/shard_map/dot_general | solution.py:51
  74.9 18.9 %slice_bitcast_fusion.3 = (f32[192,64,256]{2,0,1:T(8,128)}, f32[192,64,256]{2,0,1:T(8,128)}) fusion(f32[192,2,64,256]{3,0,2,1:T(8,128)} %fusion.2), kind=kLoop, calls=%fused_computation.19 | loop fusion | bytes 50331648 | tf_op jit(solution)/shard_map/mul | solution.py:75
  98.4 4.9 copy.46
  103.2 14.4 %fusion.25 = f32[256,4,8,4,128]{4,0,3,2,1:T(8,128)S(1)} fusion(f32[4,8,4,128,128]{4,3,2,1,0:T(8,128)S(1)} %bitcast.175, s32[128]{0:T(128)S(1)} %iota_multiply_fusion), kind=kOutput, calls=%fused_computation.45 | convolution fusion | flops 6443171840 | bytes 25166336 | tf_op jit(solution)/shard_map/...t,ut->...u/dot_general | solution.py:38
  117.7 34.2 %fusion.6 = f32[4,8,4,256,256]{4,3,2,1,0:T(8,128)} fusion(f32[256,4,8,4,128]{4,0,3,2,1:T(8,128)S(1)} %fusion.25, s32[128]{0:T(128)S(1)} %iota_multiply_fusion), kind=kOutput, calls=%fused_computation.14 | convolution fusion | flops 12885622784 | bytes 50332160 | tf_op jit(solution)/shard_map/qp,...pu->...qu/dot_general | solution.py:39
  151.9 17.5 %subtract_reduce_fusion = (f32[4,2,256,256]{2,3,1,0:T(8,128)S(1)}, f32[4,2,256,256]{2,3,1,0:T(8,128)S(1)}) fusion(f32[4,8,2,2,256,256]{4,5,3,2,1,0:T(8,128)} %bitcast.173, f32[4,8,256,256]{2,3,1,0:T(8,128)} %copy.48, f32[4,8,256,256]{2,3,1,0:T(8,128)} %copy.45), kind=kLoop, calls=%fused_computation.17 | loop fusion | flops 32505856 | bytes 54525952 | tf_op jit(solution)/shard_map/reduce_sum | solution.py:62
  171.7 5.2 copy.50
  177.0 6.9 copy.51
  183.9 6.5 all-to-all-start.1
  190.4 26.5 %fusion.4 = f32[192,2,64,256]{3,0,2,1:T(8,128)} fusion(bf16[2,64,256,316]{2,1,0,3:T(8,128)(2,1)} %bitcast.172, s32[192]{0:T(256)S(1)} %copy-done.6), kind=kOutput, calls=%fused_computation.10 | convolution fusion | flops 3976260864 | bytes 45875968 | tf_op jit(solution)/shard_map/dot_general | solution.py:51
  216.9 18.7 %slice_bitcast_fusion.5 = (f32[192,64,256]{2,0,1:T(8,128)}, f32[192,64,256]{2,0,1:T(8,128)}) fusion(f32[192,2,64,256]{3,0,2,1:T(8,128)} %fusion.4), kind=kLoop, calls=%fused_computation.21 | loop fusion | bytes 50331648 | tf_op jit(solution)/shard_map/mul | solution.py:75
  256.1 25.1 %fusion.12 = f32[192,2,2,64,256]{4,0,3,2,1:T(8,128)} fusion(f32[2,2,64,256,16]{3,2,1,0,4:T(8,128)S(1)} %bitcast.178, s32[192]{0:T(256)S(1)} %copy-done.7), kind=kOutput, calls=%fused_computation.29 | convolution fusion | flops 2415922176 | bytes 54526720 | tf_op jit(solution)/shard_map/dot_general | solution.py:49
  281.2 40.1 %multiply_subtract_fusion = (f32[192,2,1,64,256]{4,0,3,2,1:T(8,128)}, f32[192,2,1,64,256]{4,0,3,2,1:T(8,128)}) fusion(f32[192,2,2,64,256]{4,0,3,2,1:T(8,128)} %fusion.12, f32[192,64,256]{2,0,1:T(8,128)} %get-tuple-element.19, f32[192,64,256]{2,0,1:T(8,128)} %get-tuple-element.18), kind=kLoop, calls=%fused_computation.5 | loop fusion | flops 37748736 | bytes 125829120 | tf_op jit(solution)/shard_map/sub | solution.py:75
  321.3 35.1 %pad_maximum_fusion.1 = f32[192,2,2,64,256]{4,0,3,2,1:T(8,128)} fusion(f32[192,2,1,64,256]{4,0,3,2,1:T(8,128)} %get-tuple-element.15, f32[192,2,1,64,256]{4,0,3,2,1:T(8,128)} %get-tuple-element.14), kind=kLoop, calls=%fused_computation.1 | loop fusion | flops 12582912 | bytes 100663296 | tf_op jit(solution)/shard_map/stack | solution.py:77
  356.4 34.2 %copy.85 = f32[24,8,256,256]{3,1,2,0:T(8,128)} copy(f32[24,8,256,256]{3,1,0,2:T(8,128)} %bitcast.169) | data formatting | bytes 100663296
  390.6 37.5 %fusion.31 = f32[48,65536]{1,0:T(8,128)} fusion(f32[192,65536]{1,0:T(8,128)} %bitcast.167, f32[192]{0:T(256)S(1)} %copy-done.4, s32[192]{0:T(256)S(1)} %copy-done.5), kind=kOutput, calls=%fused_computation.53 | convolution fusion | flops 7247775744 | bytes 62916096 | tf_op jit(solution)/shard_map/dot_general | solution.py:83
  428.1 8.7 %fusion.72 = (f32[16,65536]{1,0:T(8,128)S(1)}, f32[16,65536]{1,0:T(8,128)}, f32[16,65536]{1,0:T(8,128)}) fusion(f32[48,65536]{1,0:T(8,128)} %fusion.31), kind=kLoop, calls=%fused_computation.97 | loop fusion | bytes 25165824 | tf_op jit(solution)/shard_map/slice | solution.py:118
  444.8 7.8 %collective-permute-start.3 = (f32[16,4,64,256]{3,0,2,1:T(8,128)}, f32[16,4,64,256]{3,0,2,1:T(8,128)}, u32[]{:S(2)}, u32[]{:S(2)}) collective-permute-start(f32[16,4,64,256]{3,0,2,1:T(8,128)} %copy.64), channel_id=1, source_target_pairs={{0,8},{4,12},{8,16},{12,20},{16,24},{20,28},{1,9},{5,13},{9,17},{1... | collective-permute-start | bytes 12582920 | tf_op jit(solution)/shard_map/ppermute | solution.py:23
  468.0 4.6 copy.79
  472.6 5.0 pad_maximum_fusion.2
  477.6 12.9 %copy.81 = f32[6,8,256,256]{3,2,1,0:T(8,128)} copy(f32[6,8,256,256]{3,1,2,0:T(8,128)} %bitcast.176) | data formatting | bytes 25165824
  490.6 34.0 %fusion.8 = f32[192,2,2,64,256]{4,0,3,2,1:T(8,128)} fusion(f32[2,2,64,256,48]{3,2,1,0,4:T(8,128)} %bitcast.174, s32[192]{0:T(256)S(1)} %copy-done.5), kind=kOutput, calls=%fused_computation.23 | convolution fusion | flops 7247766528 | bytes 62915328 | tf_op jit(solution)/shard_map/dot_general | solution.py:49
  524.6 40.3 %multiply_subtract_fusion.1 = (f32[192,2,1,64,256]{4,0,3,2,1:T(8,128)}, f32[192,2,1,64,256]{4,0,3,2,1:T(8,128)}) fusion(f32[192,2,2,64,256]{4,0,3,2,1:T(8,128)} %fusion.8, f32[192,64,256]{2,0,1:T(8,128)} %get-tuple-element.17, f32[192,64,256]{2,0,1:T(8,128)} %get-tuple-element.16), kind=kLoop, calls=%fused_computation.7 | loop fusion | flops 37748736 | bytes 125829120 | tf_op jit(solution)/shard_map/sub | solution.py:75
  564.9 34.9 %pad_maximum_fusion = f32[192,2,2,64,256]{4,0,3,2,1:T(8,128)} fusion(f32[192,2,1,64,256]{4,0,3,2,1:T(8,128)} %get-tuple-element.13, f32[192,2,1,64,256]{4,0,3,2,1:T(8,128)} %get-tuple-element.12), kind=kLoop, calls=%fused_computation | loop fusion | flops 12582912 | bytes 100663296 | tf_op jit(solution)/shard_map/stack | solution.py:77
  599.8 46.0 %copy.83 = f32[24,8,256,256]{3,2,1,0:T(8,128)} copy(f32[24,8,256,256]{3,1,0,2:T(8,128)} %bitcast.170) | data formatting | bytes 100663296
  645.8 66.0 %fusion.11 = f32[16,4,64,256]{3,0,2,1:T(8,128)S(1)} fusion(f32[16,4,64,256]{3,0,2,1:T(8,128)} %collective-permute-done.3, f32[16,4,64,256]{3,0,2,1:T(8,128)} %collective-permute-done.2, f32[16,4,64,256]{3,2,1,0:T(8,128)} %bitcast.179, f32[4,64,256,192]{2,1,0,3:T(8,128)} %bitcast.168, f32[16,192,1,1]{1,0,3,2:T(8,128)S(1)} %copy-done.2), kind=kOutput, calls=%fused_computation.28 | convolution fusion | flops 2419064832 | bytes 67121152 | tf_op jit(solution)/shard_map/dot_general | solution.py:83
  (47 shorter events, 56.4 us)
Async XLA Ops:
  0.6 6.2 copy-start.9
  0.6 97.7 %all-to-all-start = ((f32[16,8,4,32,128]{4,3,2,1,0:T(8,128)}), f32[16,8,4,32,128]{4,3,2,1,0:T(8,128)}, u32[]{:S(2)}, u32[]{:S(2)}) async-start(f32[16,8,4,32,128]{4,3,2,1,0:T(8,128)} %bitcast.192), calls=%async_computation | async-start | bytes 16777216 | tf_op jit(solution)/shard_map/all_to_all | solution.py:95
  31.2 15.8 %copy-start.8 = (s32[192]{0:T(256)S(1)}, s32[192]{0:T(256)}, u32[]{:S(2)}) copy-start(s32[192]{0:T(256)} %param.15) | copy-start | bytes 2308
  31.2 15.8 %copy-start.6 = (s32[192]{0:T(256)S(1)}, s32[192]{0:T(256)}, u32[]{:S(2)}) copy-start(s32[192]{0:T(256)} %param.14) | copy-start | bytes 2308
  31.2 16.4 %copy-start.7 = (s32[192]{0:T(256)S(1)}, s32[192]{0:T(256)}, u32[]{:S(2)}) copy-start(s32[192]{0:T(256)} %param.12) | copy-start | bytes 2308
  47.0 0.6 copy-start.3
  183.9 53.1 %all-to-all-start.1 = ((f32[4,4,256,256]{3,1,0,2:T(4,128)}), f32[4,4,256,256]{3,1,0,2:T(4,128)}, u32[]{:S(2)}, u32[]{:S(2)}) async-start(f32[4,4,256,256]{3,1,0,2:T(4,128)} %copy.51), calls=%async_computation.1 | async-start | bytes 8388608 | tf_op jit(solution)/shard_map/all_to_all | solution.py:103
  247.9 215.5 %collective-permute-start.1 = (f32[16,4,64,256]{3,2,1,0:T(8,128)}, f32[16,4,64,256]{3,2,1,0:T(8,128)}, u32[]{:S(2)}, u32[]{:S(2)}) collective-permute-start(f32[16,4,64,256]{3,2,1,0:T(8,128)} %bitcast.180), channel_id=1, source_target_pairs={{8,0},{12,4},{16,8},{20,12},{24,16},{28,20},{9,1},{13,5},{17,9},{2... | collective-permute-start | bytes 12582920 | tf_op jit(solution)/shard_map/ppermute | solution.py:23
  250.2 217.7 %collective-permute-start = (f32[16,4,64,256]{3,2,1,0:T(8,128)}, f32[16,4,64,256]{3,2,1,0:T(8,128)}, u32[]{:S(2)}, u32[]{:S(2)}) collective-permute-start(f32[16,4,64,256]{3,2,1,0:T(8,128)} %bitcast.181), channel_id=1, source_target_pairs={{4,0},{8,4},{12,8},{16,12},{20,16},{24,20},{28,24},{5,1},{9,5},{13... | collective-permute-start | bytes 12582920 | tf_op jit(solution)/shard_map/ppermute | solution.py:23
  356.4 34.2 %copy-start.4 = (f32[192]{0:T(256)S(1)}, f32[192]{0:T(256)}, u32[]{:S(2)}) copy-start(f32[192]{0:T(256)} %copy-done.3) | copy-start | bytes 2308
  356.4 34.2 %copy-start.5 = (s32[192]{0:T(256)S(1)}, s32[192]{0:T(256)}, u32[]{:S(2)}) copy-start(s32[192]{0:T(256)} %param.13) | copy-start | bytes 2308
  436.8 15.8 %copy-start.1 = (f32[16,65536]{1,0:T(8,128)S(1)}, f32[16,65536]{1,0:T(8,128)}, u32[]{:S(2)}) copy-start(f32[16,65536]{1,0:T(8,128)} %get-tuple-element.22) | copy-start | bytes 12582916
  444.8 201.1 %collective-permute-start.3 = (f32[16,4,64,256]{3,0,2,1:T(8,128)}, f32[16,4,64,256]{3,0,2,1:T(8,128)}, u32[]{:S(2)}, u32[]{:S(2)}) collective-permute-start(f32[16,4,64,256]{3,0,2,1:T(8,128)} %copy.64), channel_id=1, source_target_pairs={{0,8},{4,12},{8,16},{12,20},{16,24},{20,28},{1,9},{5,13},{9,17},{1... | collective-permute-start | bytes 12582920 | tf_op jit(solution)/shard_map/ppermute | solution.py:23
  458.2 187.6 %collective-permute-start.2 = (f32[16,4,64,256]{3,0,2,1:T(8,128)}, f32[16,4,64,256]{3,0,2,1:T(8,128)}, u32[]{:S(2)}, u32[]{:S(2)}) collective-permute-start(f32[16,4,64,256]{3,0,2,1:T(8,128)} %copy.63), channel_id=1, source_target_pairs={{0,4},{4,8},{8,12},{12,16},{16,20},{20,24},{24,28},{1,5},{5,9},{9,... | collective-permute-start | bytes 12582920 | tf_op jit(solution)/shard_map/ppermute | solution.py:23
  460.1 12.5 %copy-start = (f32[16,65536]{1,0:T(8,128)S(1)}, f32[16,65536]{1,0:T(8,128)}, u32[]{:S(2)}) copy-start(f32[16,65536]{1,0:T(8,128)} %concatenate.10) | copy-start | bytes 12582916
  599.8 46.1 %copy-start.2 = (f32[16,192,1,1]{1,0,3,2:T(8,128)S(1)}, f32[16,192,1,1]{1,0,3,2:T(8,128)}, u32[]{:S(2)}) copy-start(f32[16,192,1,1]{1,0,3,2:T(8,128)} %fusion.82) | copy-start | bytes 36868
where the time goes:
time: 727 us; the launch traced here: 717 us
  matrix products  276 us (38%)
  local copies, waits for them, and re-layouts  230 us (32%)
  other arithmetic  176 us (24%)
  starting transfers between devices  27.2 us (4%)
    unnamed x31, local copies, waits for them, and re-layouts  127 us
    dot_general x2, matrix products, collect(): return jnp.dot(onehot, terms.reshape(terms.shape[0], -1), precision=HIGHEST)  104 us
    sub x2, other arithmetic, translate(): new_real = t_real * p_real - t_imag * p_imag  80.4 us
    dot_general x4, matrix products, select_rows(): jnp.dot(onehot, flat_table, precision=HIGHEST, preferred_element_type=jnp...  70.9 us
    another operation x2, other arithmetic, translate(): return jnp.stack([new_real, new_imag], axis=-3).reshape(patterns.shape)  70 us
    dot_general x2, matrix products, select_rows(): picked = jnp.dot(onehot, flat_table, preferred_element_type=jnp.float32)  53.2 us
    mul x2, local copies, waits for them, and re-layouts, translate(): new_real = t_real * p_real - t_imag * p_imag  37.7 us
    dot_general x1, matrix products, interpolate(): return jnp.einsum('qp,...pu->...qu', phi_map, widened, precision=HIGHEST)  34.2 us
  transfers between devices with their start and end apart: 6, of which 2 were waited for; matrix products, arithmetic and copies ran while one was open for 72% of the time, Pallas kernels for 0%

commit v1 on v0

--- a/solution.py
+++ b/solution.py
@@ -1,17 +1,19 @@
+import functools
 import math
 
 import jax
 import jax.numpy as jnp
 from jax import lax
+from jax.experimental import pallas as pl
+from jax.experimental.pallas import tpu as pltpu
 from jax.sharding import PartitionSpec as P
 
-BOX_DEV = 16
 REACH = 2
-CLASSES = 316
 THETA1 = 128
 PHI1 = 128
 THETA2 = 256
 PHI2 = 256
+ROWS = 16
 
 
 HIGHEST = lax.Precision.HIGHEST
@@ -45,10 +47,7 @@
     row_ids = jnp.arange(count, dtype=jnp.int32)
     onehot = (flat_ids[:, None] == row_ids[None, :]).astype(table.dtype)
     flat_table = table.reshape(count, -1)
-    if table.dtype == jnp.float32:
-        picked = jnp.dot(onehot, flat_table, precision=HIGHEST, preferred_element_type=jnp.float32)
-    else:
-        picked = jnp.dot(onehot, flat_table, preferred_element_type=jnp.float32)
+    picked = jnp.dot(onehot, flat_table, precision=HIGHEST, preferred_element_type=jnp.float32)
     return picked.reshape(indices.shape + table.shape[1:])
 
 
@@ -66,21 +65,88 @@
     )
 
 
-def translate(table_rows, patterns):
-    shaped = patterns.reshape(patterns.shape[:-3] + (2, 2) + patterns.shape[-2:])
-    t_real = table_rows[..., 0:1, :, :]
-    t_imag = table_rows[..., 1:2, :, :]
-    p_real = shaped[..., :, 0, :, :]
-    p_imag = shaped[..., :, 1, :, :]
-    new_real = t_real * p_real - t_imag * p_imag
-    new_imag = t_imag * p_real + t_real * p_imag
-    return jnp.stack([new_real, new_imag], axis=-3).reshape(patterns.shape)
+def pair_kernel(tgt_ref, src_ref, cls_ref, live_ref, table_hbm, *rest):
+    blocks = rest[:-6]
+    out_hbm, table, sources, acc, sems, out_sem = rest[-6:]
+    box_dev = blocks[0].shape[0]
+    rows = table.shape[2]
+    copies = [pltpu.make_async_copy(table_hbm, table, sems.at[0])]
+    for b, block in enumerate(blocks):
+        copies.append(
+            pltpu.make_async_copy(block, sources.at[pl.ds(b * box_dev, box_dev)], sems.at[b + 1])
+        )
+    for c in copies:
+        c.start()
+    acc[...] = jnp.zeros_like(acc)
+    for c in copies:
+        c.wait()
+
+    def item(i, carry):
+        @pl.when(live_ref[i] != 0)
+        def _():
+            t = tgt_ref[i]
+            s = src_ref[i]
+            k = cls_ref[i]
+
+            def chunk(j, inner):
+                r0 = pl.multiple_of(j * ROWS, ROWS)
+                win = pl.ds(r0, ROWS)
+                tr = table[k, 0, win, :].astype(jnp.float32)
+                ti = table[k, 1, win, :].astype(jnp.float32)
+                for q in range(2):
+                    pr = sources[s, 2 * q, win, :]
+                    pi = sources[s, 2 * q + 1, win, :]
+                    acc[t, 2 * q, win, :] += tr * pr - ti * pi
+                    acc[t, 2 * q + 1, win, :] += ti * pr + tr * pi
+                return inner
+
+            lax.fori_loop(0, rows // ROWS, chunk, 0, unroll=True)
+
+        return carry
+
+    lax.fori_loop(0, tgt_ref.shape[0], item, 0)
+    done = pltpu.make_async_copy(acc, out_hbm, out_sem.at[0])
+    done.start()
+    done.wait()
 
 
-def collect(targets, weights, terms, count):
-    target_ids = jnp.arange(count, dtype=jnp.int32)
-    onehot = jnp.where(targets[None, :] == target_ids[:, None], weights[None, :], 0.0)
-    return jnp.dot(onehot, terms.reshape(terms.shape[0], -1), precision=HIGHEST)
+def translate_pairs(items, trans_table, blocks):
+    tgt, src, cls, live = items
+    box_dev = blocks[0].shape[0]
+    shape = blocks[0].shape
+    smem = pl.BlockSpec(memory_space=pltpu.SMEM)
+    anywhere = pl.BlockSpec(memory_space=pl.ANY)
+    return pl.pallas_call(
+        pair_kernel,
+        out_shape=jax.ShapeDtypeStruct(shape, jnp.float32),
+        in_specs=[smem] * 4 + [anywhere] * (1 + len(blocks)),
+        out_specs=anywhere,
+        scratch_shapes=[
+            pltpu.VMEM(trans_table.shape, trans_table.dtype),
+            pltpu.VMEM((len(blocks) * box_dev,) + shape[1:], jnp.float32),
+            pltpu.VMEM(shape, jnp.float32),
+            pltpu.SemaphoreType.DMA((1 + len(blocks),)),
+            pltpu.SemaphoreType.DMA((1,)),
+        ],
+        compiler_params=pltpu.CompilerParams(vmem_limit_bytes=66_000_000),
+    )(tgt, src, cls, live, trans_table, *blocks)
+
+
+def pair_items(pair_near, pair_far, pair_class, pair_live, box_dev, classes):
+    packed = jnp.stack([pair_near, pair_far, pair_class, pair_live])
+    lists = [packed] + [passed_along(packed, "box", o) for o in range(1, REACH + 1)]
+    tgt = [pair_near]
+    src = [pair_far]
+    cls = [pair_class]
+    live = [pair_live]
+    for o, lst in enumerate(lists):
+        near, far, k, alive = lst[0], lst[1], lst[2], lst[3]
+        tgt.append(far - o * box_dev)
+        base = 0 if o == 0 else (REACH + o) * box_dev
+        src.append(near + base)
+        cls.append((k + classes // 2) % classes)
+        live.append(jnp.where(far // box_dev == o, alive, 0))
+    return [jnp.concatenate(x).astype(jnp.int32) for x in (tgt, src, cls, live)]
 
 
 def body(
@@ -88,12 +154,14 @@
 ):
     dir_count = lax.axis_size("dir")
     dir_index = lax.axis_index("dir")
+    box_dev = child_pattern.shape[0] // 8
+    classes = trans_table.shape[0]
     theta_map = interp_rows(THETA1, THETA2, THETA2)
     cos_table = jnp.cos(shift_angle)
     sin_table = jnp.sin(shift_angle)
-    grouped = child_pattern.reshape(BOX_DEV, 8, 4, PHI1 // dir_count, THETA1)
+    grouped = child_pattern.reshape(box_dev, 8, 4, PHI1 // dir_count, THETA1)
     gathered = lax.all_to_all(grouped, "dir", split_axis=0, concat_axis=3, tiled=True)
-    per_dev = BOX_DEV // dir_count
+    per_dev = box_dev // dir_count
     octant_rows = lax.dynamic_slice_in_dim(octant, dir_index * (per_dev * 8), per_dev * 8).reshape(
         per_dev, 8
     )
@@ -101,25 +169,13 @@
     full_dirs = interpolate(gathered, theta_map, phi_map)
     summed = shift_sum(full_dirs, octant_rows, cos_table, sin_table)
     aggregated = lax.all_to_all(summed, "dir", split_axis=2, concat_axis=0, tiled=True)
-    table_near = select_rows(pair_class, trans_table)
-    mirror = (pair_class + CLASSES // 2) % CLASSES
-    table_far = select_rows(mirror, trans_table)
-    alive = pair_live.astype(jnp.float32)
-    to_far = translate(table_far, select_rows(pair_near, aggregated))
     blocks = [aggregated]
     for offset in range(1, REACH + 1):
         blocks.append(passed_along(aggregated, "box", -offset))
-    window = jnp.concatenate(blocks, axis=0)
-    to_near = translate(table_near, select_rows(pair_far, window))
-    incoming = collect(pair_near, alive, to_near, BOX_DEV).reshape(aggregated.shape)
-    spread = collect(pair_far, alive, to_far, (REACH + 1) * BOX_DEV).reshape(
-        (REACH + 1) * BOX_DEV, *aggregated.shape[1:]
-    )
-    incoming = incoming + spread[:BOX_DEV]
     for offset in range(1, REACH + 1):
-        incoming = incoming + passed_along(
-            spread[offset * BOX_DEV : (offset + 1) * BOX_DEV], "box", offset
-        )
+        blocks.append(passed_along(aggregated, "box", offset))
+    items = pair_items(pair_near, pair_far, pair_class, pair_live, box_dev, classes)
+    incoming = translate_pairs(items, trans_table, blocks)
     return (aggregated, incoming)
 
 

time: 727 us -> 483 us (0.66)
  the two profiles are of different devices: /device:TPU:22 before, /device:TPU:24 now
where the time goes in v1:
time: 483 us; the launch traced here: 480 us
  waiting for transfers between devices  145 us (30%)
  starting transfers between devices  108 us (22%)
  matrix products  60.3 us (12%)
  local copies, waits for them, and re-layouts  52.2 us (11%)
  blocking collectives  50.7 us (10%)
  Pallas kernels  41.9 us (9%)
  other arithmetic  21.2 us (4%)
    ppermute x6, starting transfers between devices, passed_along(): lax.ppermute(value, axis, [(source, source + steps) for source in range(f...  102 us
    ppermute x6, waiting for transfers between devices, passed_along(): lax.ppermute(value, axis, [(source, source + steps) for source in range(f...  91.7 us
    all_to_all x1, waiting for transfers between devices, body(): lax.all_to_all(grouped, 'dir', split_axis=0, concat_axis=3, tiled=True)  52.8 us
    all_to_all x1, blocking collectives, body(): lax.all_to_all(summed, 'dir', split_axis=2, concat_axis=0, tiled=True)  50.7 us
    pallas_call x1, Pallas kernels, translate_pairs(): pl.pallas_call(pair_kernel, out_shape=jax.ShapeDtypeStruct(shape, jnp.flo...  41.9 us
    dot_general x1, matrix products, interpolate(): return jnp.einsum('qp,...pu->...qu', phi_map, widened, precision=HIGHEST)  34.1 us
    dot_general x2, local copies, waits for them, and re-layouts, select_rows(): jnp.dot(onehot, flat_table, precision=HIGHEST, preferred_element_type=jnp...  20 us
    reduce_sum x1, other arithmetic, shift_sum(): new_real = jnp.sum(cosine * real_part - sine * imag_part, axis=1)  17.5 us
  transfers between devices with their start and end apart: 7, of which 3 were waited for; matrix products, arithmetic and copies ran while one was open for 9% of the time, Pallas kernels for 0%

profile of v1, /device:TPU:24, one launch (start us, length us, event | category | flops | bytes accessed | tf_op | source)
XLA Modules:
  0.0 480.0 jit_solution(15832302658596808665)
XLA Ops:
  0.6 5.7 %all-to-all-start = ((f32[16,8,4,32,128]{4,3,2,1,0:T(8,128)}), f32[16,8,4,32,128]{4,3,2,1,0:T(8,128)}, u32[]{:S(2)}, u32[]{:S(2)}) async-start(f32[16,8,4,32,128]{4,3,2,1,0:T(8,128)} %bitcast.93), calls=%async_computation | async-start | bytes 16777216 | tf_op jit(solution)/shard_map/all_to_all | solution.py:163
  6.5 8.4 %cosine_bitcast_fusion = (f32[1,8,256,256]{3,2,1,0:T(8,128)S(1)}, f32[1,8,256,256]{3,2,1,0:T(8,128)S(1)}) fusion(f32[8,256,256]{2,1,0:T(8,128)} %param.10), kind=kLoop, calls=%fused_computation.8 | loop fusion | bytes 6291456
  14.9 5.9 %fusion.12 = f32[4,8,256,256]{3,1,2,0:T(8,128)} fusion(s32[4,8]{1,0:T(4,128)S(1)} %eq.76, f32[1,8,256,256]{3,2,1,0:T(8,128)S(1)} %get-tuple-element.5), kind=kOutput, calls=%fused_computation.25 | convolution fusion | flops 201326848 | bytes 10485888 | tf_op jit(solution)/shard_map/dot_general | solution.py:50
  20.7 10.0 %copy.25 = f32[4,8,256,256]{2,3,1,0:T(8,128)} copy(f32[4,8,256,256]{3,1,2,0:T(8,128)} %fusion.12) | data formatting | bytes 16777216 | tf_op jit(solution)/shard_map/dot_general | solution.py:50
  30.7 5.9 %fusion.14 = f32[4,8,256,256]{3,1,2,0:T(8,128)} fusion(s32[4,8]{1,0:T(4,128)S(1)} %eq.76, f32[1,8,256,256]{3,2,1,0:T(8,128)S(1)} %get-tuple-element.4), kind=kOutput, calls=%fused_computation.26 | convolution fusion | flops 201326848 | bytes 10485888 | tf_op jit(solution)/shard_map/dot_general | solution.py:50
  36.6 10.1 %copy.22 = f32[4,8,256,256]{2,3,1,0:T(8,128)} copy(f32[4,8,256,256]{3,1,2,0:T(8,128)} %fusion.14) | data formatting | bytes 16777216 | tf_op jit(solution)/shard_map/dot_general | solution.py:50
  46.6 52.8 %all-to-all-done = f32[16,8,4,32,128]{4,3,2,1,0:T(8,128)} async-done(((f32[16,8,4,32,128]{4,3,2,1,0:T(8,128)}), f32[16,8,4,32,128]{4,3,2,1,0:T(8,128)}, u32[]{:S(2)}, u32[]{:S(2)}) %all-to-all-start) | async-done | bytes 8388640 | tf_op jit(solution)/shard_map/all_to_all | solution.py:163
  99.5 4.9 %copy.23 = f32[4,8,4,4,32,128]{5,4,3,2,1,0:T(8,128)S(1)} copy(f32[4,8,4,4,32,128]{5,4,2,1,0,3:T(8,128)} %bitcast.10) | data formatting | bytes 16777216 | tf_op jit(solution)/shard_map/all_to_all | solution.py:163
  104.3 14.5 %fusion.5 = f32[256,4,8,4,128]{4,0,3,2,1:T(8,128)S(1)} fusion(f32[4,8,4,128,128]{4,3,2,1,0:T(8,128)S(1)} %bitcast.84, s32[128]{0:T(128)S(1)} %iota_multiply_fusion), kind=kOutput, calls=%fused_computation.15 | convolution fusion | flops 6443171840 | bytes 25166336 | tf_op jit(solution)/shard_map/...t,ut->...u/dot_general | solution.py:40
  118.8 34.1 %fusion = f32[4,8,4,256,256]{4,3,2,1,0:T(8,128)} fusion(f32[256,4,8,4,128]{4,0,3,2,1:T(8,128)S(1)} %fusion.5, s32[128]{0:T(128)S(1)} %iota_multiply_fusion), kind=kOutput, calls=%fused_computation.2 | convolution fusion | flops 12885622784 | bytes 50332160 | tf_op jit(solution)/shard_map/qp,...pu->...qu/dot_general | solution.py:41
  152.9 17.5 %subtract_reduce_fusion = (f32[4,2,256,256]{2,3,1,0:T(8,128)S(1)}, f32[4,2,256,256]{2,3,1,0:T(8,128)S(1)}) fusion(f32[4,8,2,2,256,256]{4,5,3,2,1,0:T(8,128)} %bitcast.83, f32[4,8,256,256]{2,3,1,0:T(8,128)} %copy.25, f32[4,8,256,256]{2,3,1,0:T(8,128)} %copy.22), kind=kLoop, calls=%fused_computation.5 | loop fusion | flops 32505856 | bytes 54525952 | tf_op jit(solution)/shard_map/reduce_sum | solution.py:61
  170.5 2.3 pad_maximum_fusion
  172.7 5.2 %copy.27 = f32[4,2,2,256,256]{4,3,2,1,0:T(8,128)} copy(f32[4,2,2,256,256]{3,4,1,0,2:T(8,128)} %pad_maximum_fusion) | data formatting | bytes 8388608 | tf_op jit(solution)/shard_map/stack | solution.py:63
  178.0 4.9 %copy.28 = f32[4,4,256,256]{3,1,0,2:T(4,128)S(1)} copy(f32[4,4,256,256]{3,2,1,0:T(8,128)} %bitcast.85) | data formatting | bytes 8388608 | tf_op jit(solution)/shard_map/reshape | solution.py:63
  182.9 50.7 %all_to_all.36 = f32[4,4,256,256]{3,1,0,2:T(4,128)S(1)} all-to-all(f32[4,4,256,256]{3,1,0,2:T(4,128)S(1)} %copy.28), channel_id=1, replica_groups=mesh['box'=8,'dir'=4] {'dir'}, dimensions={2} | all-to-all | bytes 8388608 | tf_op jit(solution)/shard_map/all_to_all | solution.py:171
  233.6 2.4 copy.29
  236.1 0.5 copy.30
  236.6 3.3 collective-permute-start.2
  239.9 2.6 collective-permute-start.3
  242.5 2.5 collective-permute-start.4
  245.1 1.3 collective-permute-start.5
  246.4 1.3 collective-permute-start.1
  247.8 90.4 %collective-permute-done.1 = s32[4,192]{1,0:T(4,128)S(1)} collective-permute-done((s32[4,192]{1,0:T(4,128)S(1)}, s32[4,192]{1,0:T(4,128)S(1)}, u32[]{:S(2)}, u32[]{:S(2)}) %collective-permute-start.1) | collective-permute-done | bytes 3104 | tf_op jit(solution)/shard_map/ppermute | solution.py:25
  338.2 91.0 %collective-permute-start = (s32[4,192]{1,0:T(4,128)S(1)}, s32[4,192]{1,0:T(4,128)S(1)}, u32[]{:S(2)}, u32[]{:S(2)}) collective-permute-start(s32[4,192]{1,0:T(4,128)S(1)} %pad_add_fusion), channel_id=1, source_target_pairs={{0,4},{4,8},{8,12},{12,16},{16,20},{20,24},{24,28},{1,5},{5,9},{9,... | collective-permute-start | bytes 9224 | tf_op jit(solution)/shard_map/ppermute | solution.py:25
  429.2 1.3 collective-permute-done
  430.5 0.7 pad_add_fusion.3.cls_ref
  431.2 0.7 pad_add_fusion.2
  431.9 1.9 copy-done.1
  433.9 1.3 copy-done.2
  435.1 1.3 copy-done.3
  436.4 1.2 copy-done.4
  437.6 41.9 %shard_map.95 = f32[16,4,64,256]{3,2,1,0:T(8,128)} custom-call(s32[768]{0:T(1024)} %get-tuple-element.15.tgt_ref, s32[768]{0:T(1024)} %get-tuple-element.14.src_ref, s32[768]{0:T(1024)} %pad_add_fusion.3.cls_ref, s32[768]{0:T(1024)} %get-tuple-element.20.live_ref, bf16[316,2,64,256]{3,2,1,0:T(8,128)(2,1)} %table_hbm.1, f32[16,4,64,256]{3,2,1,0:T(8,128)} %bitcast.91, ...), custom_call_target="tpu_custom_call" | custom-call | tf_op jit(solution)/shard_map/pallas_call | solution.py:119
  (31 shorter events, 0.3 us)
Async XLA Ops:
  0.6 5.7 %copy-start.9 = (s32[128]{0:T(128)S(1)}, s32[128]{0:T(128)}, u32[]{:S(2)}) copy-start(s32[128]{0:T(128)} %param.9) | copy-start | bytes 1540
  0.6 98.8 %all-to-all-start = ((f32[16,8,4,32,128]{4,3,2,1,0:T(8,128)}), f32[16,8,4,32,128]{4,3,2,1,0:T(8,128)}, u32[]{:S(2)}, u32[]{:S(2)}) async-start(f32[16,8,4,32,128]{4,3,2,1,0:T(8,128)} %bitcast.93), calls=%async_computation | async-start | bytes 16777216 | tf_op jit(solution)/shard_map/all_to_all | solution.py:163
  236.0 10.3 %copy-start.5 = (s32[192]{0:T(256)S(1)}, s32[192]{0:T(256)}, u32[]{:S(2)}) copy-start(s32[192]{0:T(256)} %param.15) | copy-start | bytes 2308
  236.0 10.3 %copy-start.6 = (s32[192]{0:T(256)S(1)}, s32[192]{0:T(256)}, u32[]{:S(2)}) copy-start(s32[192]{0:T(256)} %param.13) | copy-start | bytes 2308
  236.0 10.3 %copy-start.7 = (s32[192]{0:T(256)S(1)}, s32[192]{0:T(256)}, u32[]{:S(2)}) copy-start(s32[192]{0:T(256)} %param.14) | copy-start | bytes 2308
  236.1 10.3 %copy-start.8 = (s32[192]{0:T(256)S(1)}, s32[192]{0:T(256)}, u32[]{:S(2)}) copy-start(s32[192]{0:T(256)} %param.12) | copy-start | bytes 2308
  236.6 8.5 %copy-start = (f32[4,4,4,64,256]{4,3,2,1,0:T(8,128)}, f32[4,4,4,64,256]{4,3,2,1,0:T(8,128)S(1)}, u32[]{:S(2)}) copy-start(f32[4,4,4,64,256]{4,3,2,1,0:T(8,128)S(1)} %copy.30) | copy-start | bytes 12582916
  236.6 195.3 %collective-permute-start.2 = (f32[16,4,64,256]{3,2,1,0:T(8,128)S(1)}, f32[16,4,64,256]{3,2,1,0:T(8,128)S(1)}, u32[]{:S(2)}, u32[]{:S(2)}) collective-permute-start(f32[16,4,64,256]{3,2,1,0:T(8,128)S(1)} %bitcast.87), channel_id=1, source_target_pairs={{4,0},{8,4},{12,8},{16,12},{20,16},{24,20},{28,24},{5,1},{9,5},{13... | collective-permute-start | bytes 12582920 | tf_op jit(solution)/shard_map/ppermute | solution.py:25
  239.9 192.0 %collective-permute-start.3 = (f32[16,4,64,256]{3,2,1,0:T(8,128)S(1)}, f32[16,4,64,256]{3,2,1,0:T(8,128)S(1)}, u32[]{:S(2)}, u32[]{:S(2)}) collective-permute-start(f32[16,4,64,256]{3,2,1,0:T(8,128)S(1)} %bitcast.88), channel_id=1, source_target_pairs={{8,0},{12,4},{16,8},{20,12},{24,16},{28,20},{9,1},{13,5},{17,9},{2... | collective-permute-start | bytes 12582920 | tf_op jit(solution)/shard_map/ppermute | solution.py:25
  242.5 189.4 %collective-permute-start.4 = (f32[16,4,64,256]{3,2,1,0:T(8,128)S(1)}, f32[16,4,64,256]{3,2,1,0:T(8,128)S(1)}, u32[]{:S(2)}, u32[]{:S(2)}) collective-permute-start(f32[16,4,64,256]{3,2,1,0:T(8,128)S(1)} %bitcast.89), channel_id=1, source_target_pairs={{0,4},{4,8},{8,12},{12,16},{16,20},{20,24},{24,28},{1,5},{5,9},{9,... | collective-permute-start | bytes 12582920 | tf_op jit(solution)/shard_map/ppermute | solution.py:25
  245.1 186.9 %collective-permute-start.5 = (f32[16,4,64,256]{3,2,1,0:T(8,128)S(1)}, f32[16,4,64,256]{3,2,1,0:T(8,128)S(1)}, u32[]{:S(2)}, u32[]{:S(2)}) collective-permute-start(f32[16,4,64,256]{3,2,1,0:T(8,128)S(1)} %bitcast.90), channel_id=1, source_target_pairs={{0,8},{4,12},{8,16},{12,20},{16,24},{20,28},{1,9},{5,13},{9,17},{1... | collective-permute-start | bytes 12582920 | tf_op jit(solution)/shard_map/ppermute | solution.py:25
  246.4 91.7 %collective-permute-start.1 = (s32[4,192]{1,0:T(4,128)S(1)}, s32[4,192]{1,0:T(4,128)S(1)}, u32[]{:S(2)}, u32[]{:S(2)}) collective-permute-start(s32[4,192]{1,0:T(4,128)S(1)} %pad_add_fusion), channel_id=1, source_target_pairs={{0,8},{4,12},{8,16},{12,20},{16,24},{20,28},{1,9},{5,13},{9,17},{1... | collective-permute-start | bytes 9224 | tf_op jit(solution)/shard_map/ppermute | solution.py:25
  338.2 92.3 %collective-permute-start = (s32[4,192]{1,0:T(4,128)S(1)}, s32[4,192]{1,0:T(4,128)S(1)}, u32[]{:S(2)}, u32[]{:S(2)}) collective-permute-start(s32[4,192]{1,0:T(4,128)S(1)} %pad_add_fusion), channel_id=1, source_target_pairs={{0,4},{4,8},{8,12},{12,16},{16,20},{20,24},{24,28},{1,5},{5,9},{9,... | collective-permute-start | bytes 9224 | tf_op jit(solution)/shard_map/ppermute | solution.py:25
  431.9 1.9 copy-start.1
  431.9 3.2 copy-start.2
  431.9 4.5 copy-start.3
  433.8 3.8 copy-start.4

commit v2 on v1

--- a/solution.py
+++ b/solution.py
@@ -65,15 +65,14 @@
     )
 
 
-def pair_kernel(tgt_ref, src_ref, cls_ref, live_ref, table_hbm, *rest):
+def pair_kernel(offsets, tgt_ref, src_ref, cls_ref, live_ref, table_hbm, *rest):
     blocks = rest[:-6]
     out_hbm, table, sources, acc, sems, out_sem = rest[-6:]
-    box_dev = blocks[0].shape[0]
     rows = table.shape[2]
     copies = [pltpu.make_async_copy(table_hbm, table, sems.at[0])]
-    for b, block in enumerate(blocks):
+    for b, (block, first) in enumerate(zip(blocks, offsets)):
         copies.append(
-            pltpu.make_async_copy(block, sources.at[pl.ds(b * box_dev, box_dev)], sems.at[b + 1])
+            pltpu.make_async_copy(block, sources.at[pl.ds(first, block.shape[0])], sems.at[b + 1])
         )
     for c in copies:
         c.start()
@@ -110,20 +109,19 @@
     done.wait()
 
 
-def translate_pairs(items, trans_table, blocks):
+def translate_pairs(items, trans_table, blocks, offsets, box_dev):
     tgt, src, cls, live = items
-    box_dev = blocks[0].shape[0]
-    shape = blocks[0].shape
+    shape = (box_dev,) + blocks[0].shape[1:]
     smem = pl.BlockSpec(memory_space=pltpu.SMEM)
     anywhere = pl.BlockSpec(memory_space=pl.ANY)
     return pl.pallas_call(
-        pair_kernel,
+        functools.partial(pair_kernel, tuple(offsets)),
         out_shape=jax.ShapeDtypeStruct(shape, jnp.float32),
         in_specs=[smem] * 4 + [anywhere] * (1 + len(blocks)),
         out_specs=anywhere,
         scratch_shapes=[
             pltpu.VMEM(trans_table.shape, trans_table.dtype),
-            pltpu.VMEM((len(blocks) * box_dev,) + shape[1:], jnp.float32),
+            pltpu.VMEM(((2 * REACH + 1) * box_dev,) + shape[1:], jnp.float32),
             pltpu.VMEM(shape, jnp.float32),
             pltpu.SemaphoreType.DMA((1 + len(blocks),)),
             pltpu.SemaphoreType.DMA((1,)),
@@ -156,26 +154,35 @@
     dir_index = lax.axis_index("dir")
     box_dev = child_pattern.shape[0] // 8
     classes = trans_table.shape[0]
+    items = pair_items(pair_near, pair_far, pair_class, pair_live, box_dev, classes)
     theta_map = interp_rows(THETA1, THETA2, THETA2)
+    phi_map = interp_rows(PHI1, PHI2, PHI2)
     cos_table = jnp.cos(shift_angle)
     sin_table = jnp.sin(shift_angle)
     grouped = child_pattern.reshape(box_dev, 8, 4, PHI1 // dir_count, THETA1)
-    gathered = lax.all_to_all(grouped, "dir", split_axis=0, concat_axis=3, tiled=True)
-    per_dev = box_dev // dir_count
-    octant_rows = lax.dynamic_slice_in_dim(octant, dir_index * (per_dev * 8), per_dev * 8).reshape(
-        per_dev, 8
-    )
-    phi_map = interp_rows(PHI1, PHI2, PHI2)
-    full_dirs = interpolate(gathered, theta_map, phi_map)
-    summed = shift_sum(full_dirs, octant_rows, cos_table, sin_table)
-    aggregated = lax.all_to_all(summed, "dir", split_axis=2, concat_axis=0, tiled=True)
-    blocks = [aggregated]
-    for offset in range(1, REACH + 1):
-        blocks.append(passed_along(aggregated, "box", -offset))
-    for offset in range(1, REACH + 1):
-        blocks.append(passed_along(aggregated, "box", offset))
-    items = pair_items(pair_near, pair_far, pair_class, pair_live, box_dev, classes)
-    incoming = translate_pairs(items, trans_table, blocks)
+    chunks = 2 if box_dev % (2 * dir_count) == 0 else 1
+    per_chunk = box_dev // chunks
+    per_dev = per_chunk // dir_count
+    parts = []
+    blocks = []
+    offsets = []
+    for c in range(chunks):
+        piece = grouped[c * per_chunk : (c + 1) * per_chunk]
+        gathered = lax.all_to_all(piece, "dir", split_axis=0, concat_axis=3, tiled=True)
+        first = (c * per_chunk + dir_index * per_dev) * 8
+        octant_rows = lax.dynamic_slice_in_dim(octant, first, per_dev * 8).reshape(per_dev, 8)
+        full_dirs = interpolate(gathered, theta_map, phi_map)
+        summed = shift_sum(full_dirs, octant_rows, cos_table, sin_table)
+        part = lax.all_to_all(summed, "dir", split_axis=2, concat_axis=0, tiled=True)
+        parts.append(part)
+        moved = [part]
+        moved += [passed_along(part, "box", -o) for o in range(1, REACH + 1)]
+        moved += [passed_along(part, "box", o) for o in range(1, REACH + 1)]
+        for b, block in enumerate(moved):
+            blocks.append(block)
+            offsets.append(b * box_dev + c * per_chunk)
+    aggregated = jnp.concatenate(parts, axis=0) if chunks > 1 else parts[0]
+    incoming = translate_pairs(items, trans_table, blocks, offsets, box_dev)
     return (aggregated, incoming)
 
 

time: 483 us -> 449 us (0.930)
  the two profiles are of different devices: /device:TPU:24 before, /device:TPU:28 now
where the time goes in v2:
time: 449 us; the launch traced here: 444 us
  waiting for transfers between devices  144 us (32%)
  matrix products  77.2 us (17%)
  local copies, waits for them, and re-layouts  64 us (14%)
  blocking collectives  51.6 us (11%)
  Pallas kernels  44.6 us (10%)
  starting transfers between devices  39.3 us (9%)
  other arithmetic  21.3 us (5%)
    ppermute x10, waiting for transfers between devices, passed_along(): lax.ppermute(value, axis, [(source, source + steps) for source in range(f...  121 us
    all_to_all x1, blocking collectives, body(): lax.all_to_all(piece, 'dir', split_axis=0, concat_axis=3, tiled=True)  51.6 us
    pallas_call x1, Pallas kernels, translate_pairs(): pl.pallas_call(functools.partial(pair_kernel, tuple(offsets)), out_shape=...  44.6 us
    dot_general x2, matrix products, interpolate(): return jnp.einsum('qp,...pu->...qu', phi_map, widened, precision=HIGHEST)  37.7 us
    ppermute x10, starting transfers between devices, passed_along(): lax.ppermute(value, axis, [(source, source + steps) for source in range(f...  26 us
    all_to_all x2, waiting for transfers between devices, body(): lax.all_to_all(summed, 'dir', split_axis=2, concat_axis=0, tiled=True)  23.1 us
    dot_general x4, local copies, waits for them, and re-layouts, select_rows(): jnp.dot(onehot, flat_table, precision=HIGHEST, preferred_element_type=jnp...  21.5 us
    dot_general x4, matrix products, select_rows(): jnp.dot(onehot, flat_table, precision=HIGHEST, preferred_element_type=jnp...  20.7 us
  transfers between devices with their start and end apart: 13, of which 5 were waited for; matrix products, arithmetic and copies ran while one was open for 25% of the time, Pallas kernels for 0%

profile of v2, /device:TPU:28, one launch (start us, length us, event | category | flops | bytes accessed | tf_op | source)
XLA Modules:
  0.0 443.6 jit_solution(5052377636565625486)
XLA Ops:
  0.6 6.9 %fusion.64 = (f32[64,4,32,128]{3,2,1,0:T(8,128)}, f32[64,4,32,128]{3,2,1,0:T(8,128)S(1)}) fusion(f32[128,4,32,128]{3,2,1,0:T(8,128)} %param.8), kind=kLoop, calls=%fused_computation.110 | loop fusion | bytes 16777216 | tf_op jit(solution)/shard_map/slice | solution.py:170
  7.5 51.6 %all_to_all.72 = f32[8,8,4,32,128]{4,3,2,1,0:T(8,128)} all-to-all(f32[8,8,4,32,128]{4,3,2,1,0:T(8,128)S(1)} %bitcast.151), channel_id=1, replica_groups=mesh['box'=8,'dir'=4] {'dir'}, dimensions={0} | all-to-all | bytes 8388608 | tf_op jit(solution)/shard_map/all_to_all | solution.py:171
  59.2 5.0 %all-to-all-start = ((f32[8,8,4,32,128]{4,3,2,1,0:T(8,128)}), f32[8,8,4,32,128]{4,3,2,1,0:T(8,128)}, u32[]{:S(2)}, u32[]{:S(2)}) async-start(f32[8,8,4,32,128]{4,3,2,1,0:T(8,128)} %bitcast.150), calls=%async_computation | async-start | bytes 8388608 | tf_op jit(solution)/shard_map/all_to_all | solution.py:171
  64.3 8.4 %cosine_bitcast_fusion = (f32[1,8,256,256]{3,2,1,0:T(8,128)S(1)}, f32[1,8,256,256]{3,2,1,0:T(8,128)S(1)}) fusion(f32[8,256,256]{2,1,0:T(8,128)} %param.10), kind=kLoop, calls=%fused_computation.16 | loop fusion | bytes 6291456
  74.1 4.8 %fusion.22 = f32[2,8,256,256]{3,1,2,0:T(8,128)} fusion(s32[2,8]{1,0:T(2,128)S(1)} %eq.134, f32[1,8,256,256]{3,2,1,0:T(8,128)S(1)} %get-tuple-element.9), kind=kOutput, calls=%fused_computation.40 | convolution fusion | flops 100663424 | bytes 6291520 | tf_op jit(solution)/shard_map/dot_general | solution.py:50
  78.9 5.3 %copy.46 = f32[2,8,256,256]{2,3,1,0:T(8,128)} copy(f32[2,8,256,256]{3,1,2,0:T(8,128)} %fusion.22) | data formatting | bytes 8388608 | tf_op jit(solution)/shard_map/dot_general | solution.py:50
  84.2 4.8 %fusion.24 = f32[2,8,256,256]{3,1,2,0:T(8,128)} fusion(s32[2,8]{1,0:T(2,128)S(1)} %eq.134, f32[1,8,256,256]{3,2,1,0:T(8,128)S(1)} %get-tuple-element.8), kind=kOutput, calls=%fused_computation.41 | convolution fusion | flops 100663424 | bytes 6291520 | tf_op jit(solution)/shard_map/dot_general | solution.py:50
  88.9 5.3 %copy.43 = f32[2,8,256,256]{2,3,1,0:T(8,128)} copy(f32[2,8,256,256]{3,1,2,0:T(8,128)} %fusion.24) | data formatting | bytes 8388608 | tf_op jit(solution)/shard_map/dot_general | solution.py:50
  94.3 6.4 %fusion.17 = f32[2,8,256,256]{3,1,2,0:T(8,128)} fusion(s32[2,8]{1,0:T(2,128)S(1)} %eq.127, f32[1,8,256,256]{3,2,1,0:T(8,128)} %copy-done), kind=kOutput, calls=%fused_computation.37 | convolution fusion | flops 100663424 | bytes 6291520 | tf_op jit(solution)/shard_map/dot_general | solution.py:50
  100.7 5.7 %copy.37 = f32[2,8,256,256]{2,3,1,0:T(8,128)} copy(f32[2,8,256,256]{3,1,2,0:T(8,128)} %fusion.17) | data formatting | bytes 8388608 | tf_op jit(solution)/shard_map/dot_general | solution.py:50
  106.4 4.8 %fusion.19 = f32[2,8,256,256]{3,1,2,0:T(8,128)} fusion(s32[2,8]{1,0:T(2,128)S(1)} %eq.127, f32[1,8,256,256]{3,2,1,0:T(8,128)S(1)} %get-tuple-element.8), kind=kOutput, calls=%fused_computation.38 | convolution fusion | flops 100663424 | bytes 6291520 | tf_op jit(solution)/shard_map/dot_general | solution.py:50
  111.1 5.3 %copy.34 = f32[2,8,256,256]{2,3,1,0:T(8,128)} copy(f32[2,8,256,256]{3,1,2,0:T(8,128)} %fusion.19) | data formatting | bytes 8388608 | tf_op jit(solution)/shard_map/dot_general | solution.py:50
  116.4 4.9 %copy.44 = f32[2,8,4,4,32,128]{5,4,3,2,1,0:T(8,128)} copy(f32[2,8,4,4,32,128]{5,4,2,1,0,3:T(8,128)} %bitcast.147) | data formatting | bytes 8388608 | tf_op jit(solution)/shard_map/all_to_all | solution.py:171
  124.0 8.1 %fusion.10 = f32[256,2,8,4,128]{4,0,3,2,1:T(8,128)S(1)} fusion(f32[2,8,4,128,128]{4,3,2,1,0:T(8,128)S(1)} %bitcast.149, s32[128]{0:T(128)S(1)} %iota_multiply_fusion), kind=kOutput, calls=%fused_computation.26 | convolution fusion | flops 3221946368 | bytes 12583424 | tf_op jit(solution)/shard_map/...t,ut->...u/dot_general | solution.py:40
  132.0 18.0 %fusion.2 = f32[2,8,4,256,256]{4,3,2,1,0:T(8,128)S(1)} fusion(f32[256,2,8,4,128]{4,0,3,2,1:T(8,128)S(1)} %fusion.10, s32[128]{0:T(128)S(1)} %iota_multiply_fusion), kind=kOutput, calls=%fused_computation.6 | convolution fusion | flops 6443171840 | bytes 25166336 | tf_op jit(solution)/shard_map/qp,...pu->...qu/dot_general | solution.py:41
  150.1 6.6 %subtract_reduce_fusion.1 = (f32[2,2,256,256]{2,3,1,0:T(8,128)S(1)}, f32[2,2,256,256]{2,3,1,0:T(8,128)}) fusion(f32[2,8,2,2,256,256]{4,5,3,2,1,0:T(8,128)S(1)} %bitcast.134, f32[2,8,256,256]{2,3,1,0:T(8,128)} %copy.37, f32[2,8,256,256]{2,3,1,0:T(8,128)} %copy.34), kind=kLoop, calls=%fused_computation.11 | loop fusion | flops 16252928 | bytes 27262976 | tf_op jit(solution)/shard_map/reduce_sum | solution.py:61
  159.9 4.3 copy.40
  164.3 3.8 all-to-all-start.1
  168.1 10.7 %fusion.7 = f32[256,2,8,4,128]{4,0,3,2,1:T(8,128)S(1)} fusion(f32[2,8,4,128,128]{4,3,2,1,0:T(8,128)} %bitcast.148, s32[128]{0:T(128)S(1)} %iota_multiply_fusion), kind=kOutput, calls=%fused_computation.23 | convolution fusion | flops 3221946368 | bytes 12583424 | tf_op jit(solution)/shard_map/...t,ut->...u/dot_general | solution.py:40
  178.8 19.7 %fusion = f32[2,8,4,256,256]{4,3,2,1,0:T(8,128)} fusion(f32[256,2,8,4,128]{4,0,3,2,1:T(8,128)S(1)} %fusion.7, s32[128]{0:T(128)S(1)} %iota_multiply_fusion), kind=kOutput, calls=%fused_computation.4 | convolution fusion | flops 6443171840 | bytes 25166336 | tf_op jit(solution)/shard_map/qp,...pu->...qu/dot_general | solution.py:41
  199.4 4.2 collective-permute-start.2
  207.5 7.9 %subtract_reduce_fusion = (f32[2,2,256,256]{2,3,1,0:T(8,128)S(1)}, f32[2,2,256,256]{2,3,1,0:T(8,128)S(1)}) fusion(f32[2,8,2,2,256,256]{4,5,3,2,1,0:T(8,128)} %bitcast.133, f32[2,8,256,256]{2,3,1,0:T(8,128)S(1)} %copy-done.3, f32[2,8,256,256]{2,3,1,0:T(8,128)S(1)} %copy-done.4), kind=kLoop, calls=%fused_computation.9 | loop fusion | flops 16252928 | bytes 27262976 | tf_op jit(solution)/shard_map/reduce_sum | solution.py:61
  217.0 2.9 copy.48
  219.9 4.3 copy.49
  224.2 4.5 %all-to-all-start.3 = ((f32[2,4,256,256]{3,1,0,2:T(4,128)}), f32[2,4,256,256]{3,1,0,2:T(4,128)}, u32[]{:S(2)}, u32[]{:S(2)}) async-start(f32[2,4,256,256]{3,1,0,2:T(4,128)} %copy.49), calls=%async_computation.3 | async-start | bytes 4194304 | tf_op jit(solution)/shard_map/all_to_all | solution.py:176
  231.3 23.1 %all-to-all-done.3 = f32[2,4,256,256]{3,1,0,2:T(4,128)} async-done(((f32[2,4,256,256]{3,1,0,2:T(4,128)}), f32[2,4,256,256]{3,1,0,2:T(4,128)}, u32[]{:S(2)}, u32[]{:S(2)}) %all-to-all-start.3) | async-done | bytes 2097184 | tf_op jit(solution)/shard_map/all_to_all | solution.py:176
  258.2 4.7 %collective-permute-start.6 = (f32[8,4,64,256]{3,2,1,0:T(8,128)S(1)}, f32[8,4,64,256]{3,2,1,0:T(8,128)S(1)}, u32[]{:S(2)}, u32[]{:S(2)}) collective-permute-start(f32[8,4,64,256]{3,2,1,0:T(8,128)S(1)} %bitcast.141), channel_id=1, source_target_pairs={{4,0},{8,4},{12,8},{16,12},{20,16},{24,20},{28,24},{5,1},{9,5},{13... | collective-permute-start | bytes 6291464 | tf_op jit(solution)/shard_map/ppermute | solution.py:25
  262.9 30.3 %collective-permute-done.2.rest_1_ = f32[8,4,64,256]{3,2,1,0:T(8,128)} collective-permute-done((f32[8,4,64,256]{3,2,1,0:T(8,128)S(1)}, f32[8,4,64,256]{3,2,1,0:T(8,128)}, u32[]{:S(2)}, u32[]{:S(2)}) %collective-permute-start.2) | collective-permute-done | bytes 2097184 | tf_op jit(solution)/shard_map/ppermute | solution.py:25
  293.2 6.8 %collective-permute-start.7 = (f32[8,4,64,256]{3,2,1,0:T(8,128)S(1)}, f32[8,4,64,256]{3,2,1,0:T(8,128)S(1)}, u32[]{:S(2)}, u32[]{:S(2)}) collective-permute-start(f32[8,4,64,256]{3,2,1,0:T(8,128)S(1)} %bitcast.142), channel_id=1, source_target_pairs={{8,0},{12,4},{16,8},{20,12},{24,16},{28,20},{9,1},{13,5},{17,9},{2... | collective-permute-start | bytes 6291464 | tf_op jit(solution)/shard_map/ppermute | solution.py:25
  308.4 74.3 %collective-permute-done.6.rest_6_ = f32[8,4,64,256]{3,2,1,0:T(8,128)S(1)} collective-permute-done((f32[8,4,64,256]{3,2,1,0:T(8,128)S(1)}, f32[8,4,64,256]{3,2,1,0:T(8,128)S(1)}, u32[]{:S(2)}, u32[]{:S(2)}) %collective-permute-start.6) | collective-permute-done | bytes 2097184 | tf_op jit(solution)/shard_map/ppermute | solution.py:25
  382.7 14.6 %collective-permute-done.9.rest_9_ = f32[8,4,64,256]{3,2,1,0:T(8,128)S(1)} collective-permute-done((f32[8,4,64,256]{3,2,1,0:T(8,128)S(1)}, f32[8,4,64,256]{3,2,1,0:T(8,128)S(1)}, u32[]{:S(2)}, u32[]{:S(2)}) %collective-permute-start.9) | collective-permute-done | bytes 2097184 | tf_op jit(solution)/shard_map/ppermute | solution.py:25
  398.6 44.6 %shard_map.95 = f32[16,4,64,256]{3,2,1,0:T(8,128)} custom-call(s32[768]{0:T(1024)} %get-tuple-element.19.tgt_ref, s32[768]{0:T(1024)} %get-tuple-element.18.src_ref, s32[768]{0:T(1024)} %pad_add_fusion.3.cls_ref, s32[768]{0:T(1024)} %get-tuple-element.26.live_ref, bf16[316,2,64,256]{3,2,1,0:T(8,128)(2,1)} %table_hbm.1, f32[8,4,64,256]{3,2,1,0:T(8,128)} %bitcast.140, ...), custom_call_target="tpu_custom_call" | custom-call | tf_op jit(solution)/shard_map/pallas_call | solution.py:117
  (69 shorter events, 29.9 us)
Async XLA Ops:
  59.2 5.0 %copy-start.14 = (s32[128]{0:T(128)S(1)}, s32[128]{0:T(128)}, u32[]{:S(2)}) copy-start(s32[128]{0:T(128)} %param.9) | copy-start | bytes 1540
  59.2 62.1 %all-to-all-start = ((f32[8,8,4,32,128]{4,3,2,1,0:T(8,128)}), f32[8,8,4,32,128]{4,3,2,1,0:T(8,128)}, u32[]{:S(2)}, u32[]{:S(2)}) async-start(f32[8,8,4,32,128]{4,3,2,1,0:T(8,128)} %bitcast.150), calls=%async_computation | async-start | bytes 8388608 | tf_op jit(solution)/shard_map/all_to_all | solution.py:171
  72.7 1.4 copy-start
  164.3 34.2 %all-to-all-start.1 = ((f32[2,4,256,256]{3,1,0,2:T(4,128)}), f32[2,4,256,256]{3,1,0,2:T(4,128)S(1)}, u32[]{:S(2)}, u32[]{:S(2)}) async-start(f32[2,4,256,256]{3,1,0,2:T(4,128)} %copy.40), calls=%async_computation.1 | async-start | bytes 4194304 | tf_op jit(solution)/shard_map/all_to_all | solution.py:176
  198.5 9.0 %copy-start.3 = (f32[2,8,256,256]{2,3,1,0:T(8,128)S(1)}, f32[2,8,256,256]{2,3,1,0:T(8,128)}, u32[]{:S(2)}) copy-start(f32[2,8,256,256]{2,3,1,0:T(8,128)} %copy.46) | copy-start | bytes 12582916
  198.5 9.0 %copy-start.4 = (f32[2,8,256,256]{2,3,1,0:T(8,128)S(1)}, f32[2,8,256,256]{2,3,1,0:T(8,128)}, u32[]{:S(2)}) copy-start(f32[2,8,256,256]{2,3,1,0:T(8,128)} %copy.43) | copy-start | bytes 12582916
  199.4 104.7 %copy-start.1 = (f32[4,2,4,64,256]{4,3,2,1,0:T(8,128)}, f32[4,2,4,64,256]{4,3,2,1,0:T(8,128)S(1)}, u32[]{:S(2)}) copy-start(f32[4,2,4,64,256]{4,3,2,1,0:T(8,128)S(1)} %copy.42) | copy-start | bytes 6291460
  199.4 93.8 %collective-permute-start.2 = (f32[8,4,64,256]{3,2,1,0:T(8,128)S(1)}, f32[8,4,64,256]{3,2,1,0:T(8,128)}, u32[]{:S(2)}, u32[]{:S(2)}) collective-permute-start(f32[8,4,64,256]{3,2,1,0:T(8,128)S(1)} %bitcast.135), channel_id=1, source_target_pairs={{4,0},{8,4},{12,8},{16,12},{20,16},{24,20},{28,24},{5,1},{9,5},{13... | collective-permute-start | bytes 6291464 | tf_op jit(solution)/shard_map/ppermute | solution.py:25
  203.6 96.4 %collective-permute-start.3 = (f32[8,4,64,256]{3,2,1,0:T(8,128)S(1)}, f32[8,4,64,256]{3,2,1,0:T(8,128)}, u32[]{:S(2)}, u32[]{:S(2)}) collective-permute-start(f32[8,4,64,256]{3,2,1,0:T(8,128)S(1)} %bitcast.136), channel_id=1, source_target_pairs={{8,0},{12,4},{16,8},{20,12},{24,16},{28,20},{9,1},{13,5},{17,9},{2... | collective-permute-start | bytes 6291464 | tf_op jit(solution)/shard_map/ppermute | solution.py:25
  206.2 95.1 %collective-permute-start.4 = (f32[8,4,64,256]{3,2,1,0:T(8,128)S(1)}, f32[8,4,64,256]{3,2,1,0:T(8,128)}, u32[]{:S(2)}, u32[]{:S(2)}) collective-permute-start(f32[8,4,64,256]{3,2,1,0:T(8,128)S(1)} %bitcast.137), channel_id=1, source_target_pairs={{0,4},{4,8},{8,12},{12,16},{16,20},{20,24},{24,28},{1,5},{5,9},{9,... | collective-permute-start | bytes 6291464 | tf_op jit(solution)/shard_map/ppermute | solution.py:25
  219.9 8.8 %copy-start.10 = (s32[192]{0:T(256)S(1)}, s32[192]{0:T(256)}, u32[]{:S(2)}) copy-start(s32[192]{0:T(256)} %param.15) | copy-start | bytes 2308
  219.9 8.8 %copy-start.11 = (s32[192]{0:T(256)S(1)}, s32[192]{0:T(256)}, u32[]{:S(2)}) copy-start(s32[192]{0:T(256)} %param.13) | copy-start | bytes 2308
  219.9 8.8 %copy-start.12 = (s32[192]{0:T(256)S(1)}, s32[192]{0:T(256)}, u32[]{:S(2)}) copy-start(s32[192]{0:T(256)} %param.14) | copy-start | bytes 2308
  219.9 8.8 %copy-start.13 = (s32[192]{0:T(256)S(1)}, s32[192]{0:T(256)}, u32[]{:S(2)}) copy-start(s32[192]{0:T(256)} %param.12) | copy-start | bytes 2308
  224.2 30.2 %all-to-all-start.3 = ((f32[2,4,256,256]{3,1,0,2:T(4,128)}), f32[2,4,256,256]{3,1,0,2:T(4,128)}, u32[]{:S(2)}, u32[]{:S(2)}) async-start(f32[2,4,256,256]{3,1,0,2:T(4,128)} %copy.49), calls=%async_computation.3 | async-start | bytes 4194304 | tf_op jit(solution)/shard_map/all_to_all | solution.py:176
  228.7 28.2 %collective-permute-start.1 = (s32[4,192]{1,0:T(4,128)S(1)}, s32[4,192]{1,0:T(4,128)S(1)}, u32[]{:S(2)}, u32[]{:S(2)}) collective-permute-start(s32[4,192]{1,0:T(4,128)S(1)} %pad_add_fusion), channel_id=1, source_target_pairs={{0,8},{4,12},{8,16},{12,20},{16,24},{20,28},{1,9},{5,13},{9,17},{1... | collective-permute-start | bytes 9224 | tf_op jit(solution)/shard_map/ppermute | solution.py:25
  230.0 28.2 %collective-permute-start = (s32[4,192]{1,0:T(4,128)S(1)}, s32[4,192]{1,0:T(4,128)S(1)}, u32[]{:S(2)}, u32[]{:S(2)}) collective-permute-start(s32[4,192]{1,0:T(4,128)S(1)} %pad_add_fusion), channel_id=1, source_target_pairs={{0,4},{4,8},{8,12},{12,16},{16,20},{20,24},{24,28},{1,5},{5,9},{9,... | collective-permute-start | bytes 9224 | tf_op jit(solution)/shard_map/ppermute | solution.py:25
  256.9 49.5 %copy-start.2 = (f32[4,2,4,64,256]{4,3,2,1,0:T(8,128)}, f32[4,2,4,64,256]{4,3,2,1,0:T(8,128)S(1)}, u32[]{:S(2)}) copy-start(f32[4,2,4,64,256]{4,3,2,1,0:T(8,128)S(1)} %copy.51) | copy-start | bytes 6291460
  256.9 51.5 %collective-permute-start.5 = (f32[8,4,64,256]{3,2,1,0:T(8,128)S(1)}, f32[8,4,64,256]{3,2,1,0:T(8,128)S(1)}, u32[]{:S(2)}, u32[]{:S(2)}) collective-permute-start(f32[8,4,64,256]{3,2,1,0:T(8,128)S(1)} %bitcast.138), channel_id=1, source_target_pairs={{0,8},{4,12},{8,16},{12,20},{16,24},{20,28},{1,9},{5,13},{9,17},{1... | collective-permute-start | bytes 6291464 | tf_op jit(solution)/shard_map/ppermute | solution.py:25
  258.2 124.4 %collective-permute-start.6 = (f32[8,4,64,256]{3,2,1,0:T(8,128)S(1)}, f32[8,4,64,256]{3,2,1,0:T(8,128)S(1)}, u32[]{:S(2)}, u32[]{:S(2)}) collective-permute-start(f32[8,4,64,256]{3,2,1,0:T(8,128)S(1)} %bitcast.141), channel_id=1, source_target_pairs={{4,0},{8,4},{12,8},{16,12},{20,16},{24,20},{28,24},{5,1},{9,5},{13... | collective-permute-start | bytes 6291464 | tf_op jit(solution)/shard_map/ppermute | solution.py:25
  293.2 89.5 %collective-permute-start.7 = (f32[8,4,64,256]{3,2,1,0:T(8,128)S(1)}, f32[8,4,64,256]{3,2,1,0:T(8,128)S(1)}, u32[]{:S(2)}, u32[]{:S(2)}) collective-permute-start(f32[8,4,64,256]{3,2,1,0:T(8,128)S(1)} %bitcast.142), channel_id=1, source_target_pairs={{8,0},{12,4},{16,8},{20,12},{24,16},{28,20},{9,1},{13,5},{17,9},{2... | collective-permute-start | bytes 6291464 | tf_op jit(solution)/shard_map/ppermute | solution.py:25
  300.0 82.7 %collective-permute-start.8 = (f32[8,4,64,256]{3,2,1,0:T(8,128)S(1)}, f32[8,4,64,256]{3,2,1,0:T(8,128)S(1)}, u32[]{:S(2)}, u32[]{:S(2)}) collective-permute-start(f32[8,4,64,256]{3,2,1,0:T(8,128)S(1)} %bitcast.143), channel_id=1, source_target_pairs={{0,4},{4,8},{8,12},{12,16},{16,20},{20,24},{24,28},{1,5},{5,9},{9,... | collective-permute-start | bytes 6291464 | tf_op jit(solution)/shard_map/ppermute | solution.py:25
  301.3 95.9 %collective-permute-start.9 = (f32[8,4,64,256]{3,2,1,0:T(8,128)S(1)}, f32[8,4,64,256]{3,2,1,0:T(8,128)S(1)}, u32[]{:S(2)}, u32[]{:S(2)}) collective-permute-start(f32[8,4,64,256]{3,2,1,0:T(8,128)S(1)} %bitcast.144), channel_id=1, source_target_pairs={{0,8},{4,12},{8,16},{12,20},{16,24},{20,28},{1,9},{5,13},{9,17},{1... | collective-permute-start | bytes 6291464 | tf_op jit(solution)/shard_map/ppermute | solution.py:25
  308.3 88.9 %copy-start.5 = (f32[8,4,64,256]{3,2,1,0:T(8,128)}, f32[8,4,64,256]{3,2,1,0:T(8,128)S(1)}, u32[]{:S(2)}) copy-start(f32[8,4,64,256]{3,2,1,0:T(8,128)S(1)} %collective-permute-done.5.rest_4_) | copy-start | bytes 6291460
  382.6 14.6 %copy-start.6 = (f32[8,4,64,256]{3,2,1,0:T(8,128)}, f32[8,4,64,256]{3,2,1,0:T(8,128)S(1)}, u32[]{:S(2)}) copy-start(f32[8,4,64,256]{3,2,1,0:T(8,128)S(1)} %collective-permute-done.6.rest_6_) | copy-start | bytes 6291460
  382.7 14.6 %copy-start.7 = (f32[8,4,64,256]{3,2,1,0:T(8,128)}, f32[8,4,64,256]{3,2,1,0:T(8,128)S(1)}, u32[]{:S(2)}) copy-start(f32[8,4,64,256]{3,2,1,0:T(8,128)S(1)} %collective-permute-done.7.rest_7_) | copy-start | bytes 6291460
  382.7 14.6 %copy-start.8 = (f32[8,4,64,256]{3,2,1,0:T(8,128)}, f32[8,4,64,256]{3,2,1,0:T(8,128)S(1)}, u32[]{:S(2)}) copy-start(f32[8,4,64,256]{3,2,1,0:T(8,128)S(1)} %collective-permute-done.8.rest_8_) | copy-start | bytes 6291460
  397.2 1.4 copy-start.9
